TPU v7x, 256 devices: a whole 4x4x8 slice. The times are simulated.
256 devices in a mesh: traj: 64 (over z, y, core), mstate: 4 (over x).
Axes of the slice: x: 4, y: 4, z: 8, core: 2. Of those that a mesh axis runs over, the one named last changes fastest.
Arguments:
- bias: float32 [32, 2097152], P(None, ('traj', 'mstate')), may hold values from -206 to 206
- labels: int32 [2097152], P(('traj', 'mstate')), may hold values from 0 to 4095, as said below
- therm_index: int32 [2097152], P(('traj', 'mstate')), may hold values from 0 to 31
- counts: int32 [32, 4096, 4096], P(None, 'traj', 'mstate'), may hold values from 0 to 4, as said below
- free_start: float32 [32, 4096], replicated, may hold values from -6 to 6
- mult_start: float32 [32, 4096], replicated, may hold values from -6 to 6
Outputs:
- free_energy: float32 [32, 4096], P(None, 'mstate')
- log_mult: float32 [32, 4096], P(None, 'mstate')
Inputs may be any that keep to these rules, and one draw needn't show every extreme that they name: `labels`: every Markov state is the label of at least one frame. `counts`: most entries are zero.
All inputs are finite; a program needn't handle non-finite values.
Results may differ from a plain program's by a relative error of at most 0.0001.
Values sent between devices are 32-bit elements; how exact they have to be, the bound alone decides.
No kernel may reach another device: no remote copies, remote signals or barrier semaphores. Data moves between devices by JAX's collectives and lax.ppermute only.
A program may use at most 64 MiB of HBM per device.

v0:
```python
import jax
import jax.numpy as jnp
from jax import lax
from jax.sharding import PartitionSpec as P

ITERS = 2


def per_device(bias, labels, therm_index, counts, free_start, mult_start):
    states_k = bias.shape[0]
    width = free_start.shape[1]
    col_count = counts.shape[1]
    row_count = counts.shape[2]
    col_start = lax.axis_index("traj") * col_count
    row_start = lax.axis_index("mstate") * row_count
    states = jax.nn.one_hot(therm_index, states_k, dtype=jnp.float32)
    local_visits = jax.ops.segment_sum(states, labels, num_segments=width).T
    visits = lax.psum(local_visits, ("traj", "mstate"))
    counts_real = counts.astype(jnp.float32)
    free, mult = (free_start, mult_start)
    for step in range(ITERS):
        free_cols = lax.dynamic_slice_in_dim(free, col_start, col_count, 1)
        mult_cols = lax.dynamic_slice_in_dim(mult, col_start, col_count, 1)
        free_rows = lax.dynamic_slice_in_dim(free, row_start, row_count, 1)
        mult_rows = lax.dynamic_slice_in_dim(mult, row_start, row_count, 1)
        weight = jax.nn.sigmoid(
            mult_rows[:, None, :]
            + free_cols[:, :, None]
            - mult_cols[:, :, None]
            - free_rows[:, None, :]
        )
        partial_rows = jnp.sum(counts_real * weight, axis=1)
        row_total = lax.psum(partial_rows, "traj")
        mult = lax.all_gather(jnp.log(0.5 + row_total), "mstate", axis=1, tiled=True)
        level = jnp.log(jnp.exp(mult) + visits) + free
        scores = jnp.take(level, labels, axis=1) - bias
        top = jnp.max(scores, axis=0)
        logl = top + jnp.log(jnp.sum(jnp.exp(scores - top[None, :]), axis=0))
        term = -bias - logl[None, :]
        shift = lax.pmax(jnp.max(term, axis=1), ("traj", "mstate"))
        weights = jnp.exp(term - shift[:, None])
        local_total = jax.ops.segment_sum(weights.T, labels, num_segments=width).T
        total = lax.psum(local_total, ("traj", "mstate"))
        free = -(shift[:, None] + jnp.log(total))
    free_out = lax.dynamic_slice_in_dim(free, row_start, row_count, 1)
    mult_out = lax.dynamic_slice_in_dim(mult, row_start, row_count, 1)
    return (free_out, mult_out)


def solution(mesh):
    placed = (
        P(None, ("traj", "mstate")),
        P(("traj", "mstate")),
        P(("traj", "mstate")),
        P(None, "traj", "mstate"),
        P(),
        P(),
    )
    return jax.shard_map(
        per_device,
        mesh=mesh,
        in_specs=placed,
        out_specs=(P(None, "mstate"), P(None, "mstate")),
        check_vma=False,
    )
```

profile of v0, /device:TPU:2, one launch (start us, length us, event | category | flops | bytes accessed | tf_op | source)
XLA Modules:
  0.0 1501.2 jit_solution(12562265268010864750)
XLA Ops:
  9.1 6.6 multiply_reduce_fusion.1
  15.8 48.6 %scatter_custom_fusion = f32[4096,32]{1,0:T(8,128)S(1)} fusion(s32[8192]{0:T(1024)S(1)} %copy-done.10, s32[8192]{0:T(1024)S(1)} %copy-done.11, f32[]{:T(128)} %constant.11.clone.1), kind=kCustom, calls=%fused_computation.11 | custom fusion | flops 786432 | bytes 557060 | tf_op jit(solution)/shard_map/scatter-add | solution.py:17
  64.4 1.4 copy.42
  65.9 2.6 copy.44
  68.5 125.1 %all-reduce.6.cloned.1.call-done = f32[32,1024]{1,0:T(8,128)} async-done(((f32[32,1024]{1,0:T(8,128)}), f32[32,1024]{1,0:T(8,128)}) %all-reduce.6.cloned.1.call-update) | async-done | bytes 131088 | tf_op jit(solution)/shard_map/psum | solution.py:33
  194.5 13.4 all_gather.6
  208.0 245.2 %all-reduce.8.cloned.1.call-done = f32[32,4096]{1,0:T(8,128)} async-done(((f32[32,4096]{1,0:T(8,128)}), f32[32,4096]{1,0:T(8,128)}) %all-reduce.8.cloned.1.call-update) | async-done | bytes 524304 | tf_op jit(solution)/shard_map/psum | solution.py:18
  453.2 2.0 log_add_fusion.1
  455.2 1.6 copy.43
  456.8 27.7 %gather_fusion = f32[8192,32]{1,0:T(8,128)} fusion(f32[32,4096]{0,1:T(8,128)S(1)} %copy.43, s32[8192]{0:T(1024)S(1)} %fusion.12), kind=kCustom, calls=%fused_computation.clone | custom fusion | bytes 2129920 | tf_op jit(solution)/shard_map/jit(_take)/gather | solution.py:36
  484.5 6.5 fusion.8
  491.1 4.0 exponential_reduce_fusion.1
  495.4 75.6 %pmax.14 = f32[32]{0:T(128)S(1)} all-reduce(f32[32]{0:T(128)S(1)} %subtract_reduce_fusion.1), channel_id=1, replica_groups=mesh['traj'=64,'mstate'=4] {'traj','mstate'}, use_global_device_ids=true, to_apply=%region_7.9 | all-reduce | flops 32 | bytes 256 | tf_op jit(solution)/shard_map/pmax | solution.py:40
  571.2 2.7 copy.45
  573.9 44.8 %scatter_custom_fusion.1 = f32[4096,32]{1,0:T(8,128)S(1)} fusion(s32[8192]{0:T(1024)S(1)} %copy-done.10, f32[8192,32]{1,0:T(8,128)} %copy.45, f32[]{:T(128)} %constant.11.clone.1), kind=kCustom, calls=%fused_computation.19 | custom fusion | flops 262144 | bytes 524800 | tf_op jit(solution)/shard_map/scatter-add | solution.py:42
  618.7 1.4 copy.46
  622.1 250.2 %all-reduce.10.cloned.1.call-done = f32[32,4096]{1,0:T(8,128)} async-done(((f32[32,4096]{1,0:T(8,128)}), f32[32,4096]{1,0:T(8,128)}) %all-reduce.10.cloned.1.call-update) | async-done | bytes 524304 | tf_op jit(solution)/shard_map/psum | solution.py:43
  872.3 1.2 add_negate_fusion
  873.6 6.7 multiply_reduce_fusion
  880.4 173.8 %all-reduce.12.cloned.1.call-done = f32[32,1024]{1,0:T(8,128)} async-done(((f32[32,1024]{1,0:T(8,128)}), f32[32,1024]{1,0:T(8,128)}) %all-reduce.12.cloned.1.call-update) | async-done | bytes 131088 | tf_op jit(solution)/shard_map/psum | solution.py:33
  1055.1 13.4 all_gather.7
  1069.4 1.0 log_add_fusion
  1070.4 1.6 copy.47
  1072.1 27.7 %gather_fusion.1 = f32[8192,32]{1,0:T(8,128)} fusion(f32[32,4096]{0,1:T(8,128)S(1)} %copy.47, s32[8192]{0:T(1024)S(1)} %fusion.12), kind=kCustom, calls=%fused_computation.1.clone | custom fusion | bytes 2129920 | tf_op jit(solution)/shard_map/jit(_take)/gather | solution.py:36
  1099.8 6.5 fusion.9
  1106.4 4.0 exponential_reduce_fusion
  1110.6 73.3 %pmax.15 = f32[32]{0:T(128)S(1)} all-reduce(f32[32]{0:T(128)S(1)} %subtract_reduce_fusion), channel_id=1, replica_groups=mesh['traj'=64,'mstate'=4] {'traj','mstate'}, use_global_device_ids=true, to_apply=%region_15.17 | all-reduce | flops 32 | bytes 256 | tf_op jit(solution)/shard_map/pmax | solution.py:40
  1184.2 2.6 copy.49
  1186.8 45.7 %scatter_custom_fusion.2 = f32[4096,32]{1,0:T(8,128)} fusion(s32[8192]{0:T(1024)S(1)} %copy-done.10, f32[8192,32]{1,0:T(8,128)} %copy.49, f32[]{:T(128)} %constant.11.clone.1), kind=kCustom, calls=%fused_computation.17 | custom fusion | flops 262144 | bytes 524800 | tf_op jit(solution)/shard_map/scatter-add | solution.py:42
  1232.5 1.6 constant_dynamic-slice_fusion
  1234.1 258.6 %all-reduce.14.cloned.1.call-done = f32[32,4096]{0,1:T(8,128)} async-done(((f32[32,4096]{0,1:T(8,128)}), f32[32,4096]{0,1:T(8,128)}) %all-reduce.14.cloned.1.call-update) | async-done | bytes 524304 | tf_op jit(solution)/shard_map/psum | solution.py:43
  1492.7 1.1 fusion.11
  (51 shorter events, 8.6 us)
Async XLA Ops:
  7.2 186.5 %all-reduce.6.cloned.1.call-start = ((), (), s32[]{:S(2)}) async-start(), calls=%async_computation | async-start | bytes 262144 | tf_op jit(solution)/shard_map/psum | solution.py:33
  9.0 6.7 copy-start.10
  9.0 6.7 copy-start.11
  15.7 50.2 %copy-start.2 = (f32[32,8192]{1,0:T(8,128)S(1)}, f32[32,8192]{1,0:T(8,128)}, u32[]{:S(2)}) copy-start(f32[32,8192]{1,0:T(8,128)} %param.8) | copy-start | bytes 3145732
  15.7 437.5 %all-reduce.8.cloned.1.call-start = ((), (), s32[]{:S(2)}) async-start(), calls=%async_computation.1 | async-start | bytes 1048576 | tf_op jit(solution)/shard_map/psum | solution.py:18
  65.8 387.4 %copy-start.9 = (f32[32,4096]{1,0:T(8,128)S(1)}, f32[32,4096]{1,0:T(8,128)}, u32[]{:S(2)}) copy-start(f32[32,4096]{1,0:T(8,128)} %param.12) | copy-start | bytes 1572868
  65.8 806.5 %all-reduce.10.cloned.1.call-start = ((), (), s32[]{:S(2)}) async-start(), calls=%async_computation.2 | async-start | bytes 1048576 | tf_op jit(solution)/shard_map/psum | solution.py:43
  208.0 245.2 %copy-start.5 = (f32[32,4096]{1,0:T(8,128)}, f32[32,4096]{1,0:T(8,128)S(1)}, u32[]{:S(2)}) copy-start(f32[32,4096]{1,0:T(8,128)S(1)} %all_gather.6) | copy-start | bytes 1572868
  484.5 6.5 copy-start
  484.5 6.5 copy-start.4
  620.1 434.0 %all-reduce.12.cloned.1.call-start = ((), (), s32[]{:S(2)}) async-start(), calls=%async_computation.3 | async-start | bytes 262144 | tf_op jit(solution)/shard_map/psum | solution.py:33
  873.5 195.9 %copy-start.7 = (f32[32,4096]{1,0:T(8,128)S(1)}, f32[32,4096]{1,0:T(8,128)}, u32[]{:S(2)}) copy-start(f32[32,4096]{1,0:T(8,128)} %all-reduce.10.cloned.1.call-done) | copy-start | bytes 1572868
  873.5 195.8 %copy-start.8 = (f32[32,4096]{1,0:T(8,128)S(1)}, f32[32,4096]{1,0:T(8,128)}, u32[]{:S(2)}) copy-start(f32[32,4096]{1,0:T(8,128)} %all-reduce.8.cloned.1.call-done) | copy-start | bytes 1572868
  880.3 612.4 %all-reduce.14.cloned.1.call-start = ((), (), s32[]{:S(2)}) async-start(), calls=%async_computation.4 | async-start | bytes 4194304 | tf_op jit(solution)/shard_map/psum | solution.py:43
  1068.5 0.9 copy-start.6
  1099.8 6.5 copy-start.1
  1099.8 6.5 copy-start.3
Sparse Core Ops, SparseCore 0:
  15.8 177.7 all-reduce.5
  199.1 254.0 all-reduce.7
  620.2 251.9 all-reduce.9
  880.4 173.6 all-reduce.11
  1232.7 260.0 all-reduce.13
where the time goes:
time: 1500 us
  waiting for transfers between devices  1050 us (70%)
  other arithmetic  182 us (12%)
  blocking collectives  176 us (12%)
  local copies, waits for them, and re-layouts  76.4 us (5%)
    psum x2, waiting for transfers between devices, per_device(): total = lax.psum(local_total, ('traj', 'mstate'))  509 us
    psum x2, waiting for transfers between devices, per_device(): row_total = lax.psum(partial_rows, 'traj')  299 us
    psum x1, waiting for transfers between devices, per_device(): visits = lax.psum(local_visits, ('traj', 'mstate'))  245 us
    pmax x2, blocking collectives, per_device(): shift = lax.pmax(jnp.max(term, axis=1), ('traj', 'mstate'))  149 us
    scatter-add x2, other arithmetic, per_device(): local_total = jax.ops.segment_sum(weights.T, labels, num_segments=width).T  90.5 us
    gather x2, local copies, waits for them, and re-layouts, per_device(): scores = jnp.take(level, labels, axis=1) - bias  55.5 us
    scatter-add x1, other arithmetic, per_device(): local_visits = jax.ops.segment_sum(states, labels, num_segments=width).T  48.6 us
  transfers between devices with their start and end apart: 5, of which 5 were waited for; matrix products, arithmetic and copies ran while one was open for 4% of the time, Pallas kernels for 0%

commit v1 on v0

--- a/solution.py
+++ b/solution.py
@@ -30,7 +30,8 @@
             - free_rows[:, None, :]
         )
         partial_rows = jnp.sum(counts_real * weight, axis=1)
-        row_total = lax.psum(partial_rows, "traj")
+        terms = lax.all_gather(partial_rows, "traj")
+        row_total = jnp.sum(terms, axis=0)
         mult = lax.all_gather(jnp.log(0.5 + row_total), "mstate", axis=1, tiled=True)
         level = jnp.log(jnp.exp(mult) + visits) + free
         scores = jnp.take(level, labels, axis=1) - bias

time: 1500 us -> 1290 us (0.86)
  waiting for transfers between devices: 1050 us -> 834 us
    psum x2 -> x0, waiting for transfers between devices: 299 us -> none  [per_device(): row_total = lax.psum(partial_rows, 'traj')]
    all_gather x0 -> x2, waiting for transfers between devices: none -> 115 us  [per_device(): terms = lax.all_gather(partial_rows, 'traj')]
    psum x1, waiting for transfers between devices: 245 us -> 209 us  [per_device(): visits = lax.psum(local_visits, ('traj', 'mstate'))]
  transfers between devices with their start and end apart: 5 -> 5, of which waited for: 5 -> 5; matrix products, arithmetic and copies ran while one was open for 4% -> 5% of each run, Pallas kernels for 0% -> 0%
where the time goes in v1:
time: 1290 us
  waiting for transfers between devices  834 us (65%)
  other arithmetic  188 us (15%)
  blocking collectives  174 us (13%)
  local copies, waits for them, and re-layouts  76.3 us (6%)
  between operations  15.9 us (1%)
    psum x2, waiting for transfers between devices, per_device(): total = lax.psum(local_total, ('traj', 'mstate'))  509 us
    psum x1, waiting for transfers between devices, per_device(): visits = lax.psum(local_visits, ('traj', 'mstate'))  209 us
    pmax x2, blocking collectives, per_device(): shift = lax.pmax(jnp.max(term, axis=1), ('traj', 'mstate'))  148 us
    all_gather x2, waiting for transfers between devices, per_device(): terms = lax.all_gather(partial_rows, 'traj')  115 us
    scatter-add x2, other arithmetic, per_device(): local_total = jax.ops.segment_sum(weights.T, labels, num_segments=width).T  90.5 us
    gather x2, local copies, waits for them, and re-layouts, per_device(): scores = jnp.take(level, labels, axis=1) - bias  55.4 us
    scatter-add x1, other arithmetic, per_device(): local_visits = jax.ops.segment_sum(states, labels, num_segments=width).T  48.6 us
    all_gather x2, blocking collectives, per_device(): lax.all_gather(jnp.log(0.5 + row_total), 'mstate', axis=1, tiled=True)  26.4 us
  transfers between devices with their start and end apart: 5, of which 5 were waited for; matrix products, arithmetic and copies ran while one was open for 5% of the time, Pallas kernels for 0%

profile of v1, /device:TPU:2, one launch (start us, length us, event | category | flops | bytes accessed | tf_op | source)
XLA Modules:
  0.0 1288.3 jit_solution(11508771814225955957)
XLA Ops:
  9.9 6.6 multiply_reduce_fusion.1
  16.6 48.6 %scatter_custom_fusion = f32[4096,32]{1,0:T(8,128)S(1)} fusion(s32[8192]{0:T(1024)S(1)} %copy-done.10, s32[8192]{0:T(1024)S(1)} %copy-done.11, f32[]{:T(128)} %constant.11.clone.1), kind=kCustom, calls=%fused_computation.11 | custom fusion | flops 786432 | bytes 557060 | tf_op jit(solution)/shard_map/scatter-add | solution.py:17
  65.2 1.4 copy.42
  66.8 2.7 copy.44
  69.5 33.3 %all-gather.5.cloned.1.call-done = f32[2048,1024]{1,0:T(8,128)} async-done(((f32[32,1024]{1,0:T(8,128)}), f32[2048,1024]{1,0:T(8,128)}) %all-gather.5.cloned.1.call-update) | async-done | bytes 8388624 | tf_op jit(solution)/shard_map/all_gather | solution.py:33
  102.8 4.0 reduce_sum.55
  106.8 13.0 %all_gather.20 = f32[32,4096]{1,0:T(8,128)S(1)} all-gather(f32[32,1024]{1,0:T(8,128)S(1)} %add_log_fusion.1), channel_id=1, replica_groups=mesh['traj'=64,'mstate'=4] {'mstate'}, dimensions={1}, use_global_device_ids=true | all-gather | bytes 655360 | tf_op jit(solution)/shard_map/all_gather | solution.py:35
  119.8 209.4 %all-reduce.4.cloned.1.call-done = f32[32,4096]{1,0:T(8,128)} async-done(((f32[32,4096]{1,0:T(8,128)}), f32[32,4096]{1,0:T(8,128)}) %all-reduce.4.cloned.1.call-update) | async-done | bytes 524304 | tf_op jit(solution)/shard_map/psum | solution.py:18
  329.2 2.0 log_add_fusion.1
  331.2 1.6 copy.43
  332.8 27.7 %gather_fusion = f32[8192,32]{1,0:T(8,128)} fusion(f32[32,4096]{0,1:T(8,128)S(1)} %copy.43, s32[8192]{0:T(1024)S(1)} %fusion.12), kind=kCustom, calls=%fused_computation.clone | custom fusion | bytes 2129920 | tf_op jit(solution)/shard_map/jit(_take)/gather | solution.py:37
  360.5 6.5 fusion.8
  367.1 4.0 exponential_reduce_fusion.1
  371.3 75.6 %pmax.14 = f32[32]{0:T(128)S(1)} all-reduce(f32[32]{0:T(128)S(1)} %subtract_reduce_fusion.1), channel_id=1, replica_groups=mesh['traj'=64,'mstate'=4] {'traj','mstate'}, use_global_device_ids=true, to_apply=%region_7.9 | all-reduce | flops 32 | bytes 256 | tf_op jit(solution)/shard_map/pmax | solution.py:41
  447.2 2.6 copy.45
  449.8 44.8 %scatter_custom_fusion.1 = f32[4096,32]{1,0:T(8,128)S(1)} fusion(s32[8192]{0:T(1024)S(1)} %copy-done.10, f32[8192,32]{1,0:T(8,128)} %copy.45, f32[]{:T(128)} %constant.11.clone.1), kind=kCustom, calls=%fused_computation.19 | custom fusion | flops 262144 | bytes 524800 | tf_op jit(solution)/shard_map/scatter-add | solution.py:43
  494.6 1.4 copy.46
  498.0 249.8 %all-reduce.6.cloned.1.call-done = f32[32,4096]{1,0:T(8,128)} async-done(((f32[32,4096]{1,0:T(8,128)}), f32[32,4096]{1,0:T(8,128)}) %all-reduce.6.cloned.1.call-update) | async-done | bytes 524304 | tf_op jit(solution)/shard_map/psum | solution.py:44
  747.8 1.2 add_negate_fusion
  749.0 6.7 multiply_reduce_fusion
  755.8 81.9 %all-gather.7.cloned.1.call-done = f32[2048,1024]{1,0:T(8,128)} async-done(((f32[32,1024]{1,0:T(8,128)}), f32[2048,1024]{1,0:T(8,128)}) %all-gather.7.cloned.1.call-update) | async-done | bytes 8388624 | tf_op jit(solution)/shard_map/all_gather | solution.py:33
  837.7 4.0 reduce_sum.58
  841.7 13.4 %all_gather.23 = f32[32,4096]{1,0:T(8,128)S(1)} all-gather(f32[32,1024]{1,0:T(8,128)S(1)} %add_log_fusion), channel_id=1, replica_groups=mesh['traj'=64,'mstate'=4] {'mstate'}, dimensions={1}, use_global_device_ids=true | all-gather | bytes 655360 | tf_op jit(solution)/shard_map/all_gather | solution.py:35
  856.9 1.6 copy.47
  858.6 27.7 %gather_fusion.1 = f32[8192,32]{1,0:T(8,128)} fusion(f32[32,4096]{0,1:T(8,128)S(1)} %copy.47, s32[8192]{0:T(1024)S(1)} %fusion.12), kind=kCustom, calls=%fused_computation.1.clone | custom fusion | bytes 2129920 | tf_op jit(solution)/shard_map/jit(_take)/gather | solution.py:37
  886.3 6.5 fusion.9
  892.8 4.0 exponential_reduce_fusion
  897.1 72.3 %pmax.15 = f32[32]{0:T(128)S(1)} all-reduce(f32[32]{0:T(128)S(1)} %subtract_reduce_fusion), channel_id=1, replica_groups=mesh['traj'=64,'mstate'=4] {'traj','mstate'}, use_global_device_ids=true, to_apply=%region_15.17 | all-reduce | flops 32 | bytes 256 | tf_op jit(solution)/shard_map/pmax | solution.py:41
  969.6 2.6 copy.49
  972.2 45.7 %scatter_custom_fusion.2 = f32[4096,32]{1,0:T(8,128)} fusion(s32[8192]{0:T(1024)S(1)} %copy-done.10, f32[8192,32]{1,0:T(8,128)} %copy.49, f32[]{:T(128)} %constant.11.clone.1), kind=kCustom, calls=%fused_computation.17 | custom fusion | flops 262144 | bytes 524800 | tf_op jit(solution)/shard_map/scatter-add | solution.py:43
  1017.9 1.6 constant_dynamic-slice_fusion
  1019.5 259.3 %all-reduce.8.cloned.1.call-done = f32[32,4096]{0,1:T(8,128)} async-done(((f32[32,4096]{0,1:T(8,128)}), f32[32,4096]{0,1:T(8,128)}) %all-reduce.8.cloned.1.call-update) | async-done | bytes 524304 | tf_op jit(solution)/shard_map/psum | solution.py:44
  (53 shorter events, 8.9 us)
Async XLA Ops:
  8.0 94.8 %all-gather.5.cloned.1.call-start = ((), (), s32[]{:S(2)}) async-start(), calls=%async_computation.3 | async-start | bytes 8519680 | tf_op jit(solution)/shard_map/all_gather | solution.py:33
  9.9 6.7 copy-start.10
  9.9 6.7 copy-start.11
  16.5 50.3 %copy-start.2 = (f32[32,8192]{1,0:T(8,128)S(1)}, f32[32,8192]{1,0:T(8,128)}, u32[]{:S(2)}) copy-start(f32[32,8192]{1,0:T(8,128)} %param.8) | copy-start | bytes 3145732
  16.5 312.6 %all-reduce.4.cloned.1.call-start = ((), (), s32[]{:S(2)}) async-start(), calls=%async_computation | async-start | bytes 1048576 | tf_op jit(solution)/shard_map/psum | solution.py:18
  66.7 681.1 %all-reduce.6.cloned.1.call-start = ((), (), s32[]{:S(2)}) async-start(), calls=%async_computation.1 | async-start | bytes 1048576 | tf_op jit(solution)/shard_map/psum | solution.py:44
  102.8 226.4 %copy-start.9 = (f32[32,4096]{1,0:T(8,128)S(1)}, f32[32,4096]{1,0:T(8,128)}, u32[]{:S(2)}) copy-start(f32[32,4096]{1,0:T(8,128)} %param.12) | copy-start | bytes 1572868
  119.8 209.4 %copy-start.5 = (f32[32,4096]{1,0:T(8,128)}, f32[32,4096]{1,0:T(8,128)S(1)}, u32[]{:S(2)}) copy-start(f32[32,4096]{1,0:T(8,128)S(1)} %all_gather.20) | copy-start | bytes 1572868
  360.5 6.5 copy-start
  360.5 6.5 copy-start.4
  496.0 341.6 %all-gather.7.cloned.1.call-start = ((), (), s32[]{:S(2)}) async-start(), calls=%async_computation.4 | async-start | bytes 8519680 | tf_op jit(solution)/shard_map/all_gather | solution.py:33
  755.7 523.1 %all-reduce.8.cloned.1.call-start = ((), (), s32[]{:S(2)}) async-start(), calls=%async_computation.2 | async-start | bytes 4194304 | tf_op jit(solution)/shard_map/psum | solution.py:44
  837.7 18.2 %copy-start.7 = (f32[32,4096]{1,0:T(8,128)S(1)}, f32[32,4096]{1,0:T(8,128)}, u32[]{:S(2)}) copy-start(f32[32,4096]{1,0:T(8,128)} %all-reduce.6.cloned.1.call-done) | copy-start | bytes 1572868
  837.7 18.2 %copy-start.8 = (f32[32,4096]{1,0:T(8,128)S(1)}, f32[32,4096]{1,0:T(8,128)}, u32[]{:S(2)}) copy-start(f32[32,4096]{1,0:T(8,128)} %all-reduce.4.cloned.1.call-done) | copy-start | bytes 1572868
  855.1 0.8 copy-start.6
  886.3 6.5 copy-start.1
  886.3 6.5 copy-start.3
Sparse Core Ops, SparseCore 0:
  16.6 86.0 all-gather.4
  755.8 81.8 all-gather.6
Sparse Core Ops, SparseCore 1:
  66.8 262.3 all-reduce.3
  496.1 251.6 all-reduce.5
  1018.0 260.7 all-reduce.7
